TPU v7x, 512 devices: a whole 4x4x16 slice. The times are simulated.
512 devices in a mesh: sub: 128 (over z, x, core), crow: 4 (over y).
Axes of the slice: x: 4, y: 4, z: 16, core: 2. Of those that a mesh axis runs over, the one named last changes fastest.
Arguments:
- deflation: bfloat16 [128, 12288, 128], P('sub', 'crow'), as said below
- diag_op: bfloat16 [128, 96, 128, 128], P('sub', 'crow'), as said below
- upper_op: bfloat16 [128, 96, 128, 128], P('sub', 'crow'), may hold values from -0.022094727 to 0.022094727
- tile_blocks: int32 [128, 4, 16], P('sub', 'crow'), may hold values from 0 to 23
- pair_counts: int32 [128, 8], P('sub'), may hold values from 0 to 8, as said below
- pivot_owner: int32 [128], P('sub'), may hold values from 0 to 3
Outputs:
- schur_self: float32 [16384, 128], P(('sub', 'crow'))
- schur_coupling: float32 [16384, 1024], P(('sub', 'crow'))
- panel: float32 [16384, 32], P(('sub', 'crow'))
Inputs may be any that keep to these rules, and one draw needn't show every extreme that they name: deflation has independent columns of different scales. Each diag_op block is symmetric with a positive diagonal, and every A_s is symmetric positive definite. pair_counts[s, j] equals pair_counts[s + o[j], 7 - j], is 0 where s + o[j] lies outside 0 to 127, and the pair of subdomains 0 and 1 shares 8 tiles.
All inputs are finite; a program needn't handle non-finite values.
Results may differ from a plain program's by a relative error of at most 0.0029.
Values may be sent and summed in bfloat16 or wider, within the bound.
No kernel may reach another device: no remote copies, remote signals or barrier semaphores. Data moves between devices by JAX's collectives and lax.ppermute only.
A program may use at most 64 MiB of HBM per device.

v0:
```python
import jax
import jax.numpy as jnp
from jax import lax
from jax.sharding import PartitionSpec as P


def padded_2(block, sides, width):
    for axis, dim in sides:
        count = lax.axis_size(axis)
        forward = [(i, i + 1) for i in range(count - 1)]
        backward = [(target, source) for source, target in forward]
        low = lax.ppermute(
            lax.slice_in_dim(block, block.shape[dim] - width, None, axis=dim), axis, forward
        )
        high = lax.ppermute(lax.slice_in_dim(block, 0, width, axis=dim), axis, backward)
        block = jnp.concatenate([low, block, high], axis=dim)
    return block


def shifted(value, axis, steps):
    count = lax.axis_size(axis)
    initial, last = (max(0, -steps), min(count, count - steps))
    return lax.ppermute(value, axis, [(source, source + steps) for source in range(initial, last)])


def broadcast(shard, axis, root):
    mine = lax.axis_index(axis) == root
    return lax.psum(jnp.where(mine, shard, jnp.zeros_like(shard)), axis)


def neighbour_offsets(across):
    return [-across - 1, -across, -across + 1, -1, 1, across - 1, across, across + 1]


def per_device(deflation, diag_op, upper_op, tile_blocks, pair_counts, pivot_owner):
    crow_count = lax.axis_size("crow")
    crow_place = lax.axis_index("crow")
    sub_count = lax.axis_size("sub")
    across = min(16, sub_count // 2)
    offsets = neighbour_offsets(across)
    local_rows = deflation[0]
    blocks_here, tile_rows = (diag_op.shape[1], diag_op.shape[2])
    coarse_width = local_rows.shape[1]
    slot_count = pair_counts.shape[1]
    per_slot = tile_blocks.shape[2] // slot_count
    padded = padded_2(local_rows, (("crow", 0),), tile_rows)
    stacked = padded.reshape(blocks_here + 2, tile_rows, coarse_width)
    centre = stacked[1:-1]
    previous_upper = shifted(upper_op[0, blocks_here - 1], "crow", 1)
    lower_blocks = jnp.concatenate([previous_upper[None], upper_op[0, :-1]], 0)
    product = (
        jnp.einsum("bij,bjk->bik", diag_op[0], centre, preferred_element_type=jnp.float32)
        + jnp.einsum("bij,bjk->bik", upper_op[0], stacked[2:], preferred_element_type=jnp.float32)
        + jnp.einsum("bji,bjk->bik", lower_blocks, stacked[:-2], preferred_element_type=jnp.float32)
    )
    applied = product.astype(jnp.bfloat16)
    chosen = tile_blocks[0, 0]
    own_tiles = centre[chosen].reshape(slot_count, per_slot, tile_rows, coarse_width)
    outgoing = applied[chosen].reshape(slot_count, per_slot, tile_rows, coarse_width)
    position = crow_place * per_slot + jnp.arange(per_slot, dtype=jnp.int32)
    live_mask = (position[None, :] < pair_counts[0][:, None]).astype(jnp.bfloat16)
    own_masked = own_tiles * live_mask[:, :, None, None]
    arrived = [None] * slot_count
    for slot_index in range(slot_count):
        arrived[slot_index] = shifted(
            outgoing[slot_count - 1 - slot_index], "sub", -offsets[slot_index]
        )
    received = jnp.stack(arrived)
    flat_vectors = centre.reshape(blocks_here * tile_rows, coarse_width)
    flat_applied = applied.reshape(blocks_here * tile_rows, coarse_width)
    row_share = coarse_width // crow_count
    owner_index = pivot_owner[0]
    gram_part = jnp.einsum(
        "nr,nk->rk", flat_vectors, flat_applied, preferred_element_type=jnp.float32
    )
    coupling = jnp.einsum(
        "jutr,jutk->rjk", own_masked, received, preferred_element_type=jnp.float32
    )
    own_rows = lax.psum_scatter(
        jnp.concatenate([gram_part[:, None, :], coupling], 1).reshape(
            row_share * lax.axis_size("crow"), (slot_count + 1) * coarse_width
        ),
        "crow",
        scatter_dimension=0,
        tiled=True,
    )
    leading = broadcast(own_rows, "crow", owner_index)
    pivot_block = lax.dynamic_slice_in_dim(leading, owner_index * row_share, row_share, 1)
    factor = jnp.linalg.cholesky(pivot_block)
    solved = jax.scipy.linalg.solve_triangular(factor, leading, lower=True)
    columns = lax.dynamic_slice_in_dim(own_rows, owner_index * row_share, row_share, 1)
    panel_rows = jax.scipy.linalg.solve_triangular(factor, columns.T, lower=True).T
    updated = own_rows - jnp.dot(panel_rows, solved, precision=lax.Precision.HIGHEST)
    return (updated[:, :coarse_width], updated[:, coarse_width:], panel_rows)


def solution(mesh):
    placed = (
        P("sub", "crow", None),
        P("sub", "crow", None, None),
        P("sub", "crow", None, None),
        P("sub", "crow", None),
        P("sub", None),
        P("sub"),
    )
    return jax.shard_map(
        per_device,
        mesh=mesh,
        in_specs=placed,
        out_specs=(P(("sub", "crow"), None), P(("sub", "crow"), None), P(("sub", "crow"), None)),
        check_vma=False,
    )
```

profile of v0, /device:TPU:2, one launch (start us, length us, event | category | flops | bytes accessed | tf_op | source)
XLA Modules:
  0.0 182.8 jit_solution(14846364270615309179)
XLA Ops:
  8.1 1.3 collective-permute-start
  9.4 4.5 %collective-permute-start.2 = (bf16[128,128]{1,0:T(8,128)(2,1)S(1)}, bf16[128,128]{1,0:T(8,128)(2,1)S(1)}, u32[]{:S(2)}, u32[]{:S(2)}) collective-permute-start(bf16[128,128]{1,0:T(8,128)(2,1)S(1)} %get-tuple-element.11), channel_id=1, source_target_pairs={{0,1},{1,2},{2,3},{4,5},{5,6},{6,7},{8,9},{9,10},{10,11},{12,13},{... | collective-permute-start | bytes 98312 | tf_op jit(solution)/shard_map/ppermute | solution.py:12
  14.8 3.5 %collective-permute-start.1 = (bf16[128,128]{0,1:T(8,128)(2,1)S(1)}, bf16[128,128]{0,1:T(8,128)(2,1)S(1)}, u32[]{:S(2)}, u32[]{:S(2)}) collective-permute-start(bf16[128,128]{0,1:T(8,128)(2,1)S(1)} %bitcast.93), channel_id=1, source_target_pairs={{0,1},{1,2},{2,3},{4,5},{5,6},{6,7},{8,9},{9,10},{10,11},{12,13},{... | collective-permute-start | bytes 98312 | tf_op jit(solution)/shard_map/ppermute | solution.py:23
  19.0 1.6 fusion.7
  21.6 2.3 %copy.28 = bf16[1,23,128,128]{2,3,1,0:T(8,128)(2,1)} copy(bf16[1,23,128,128]{3,2,1,0:T(8,128)(2,1)} %slice.98) | data formatting | bytes 1507328
  23.9 1.4 gather_fusion.1
  27.6 1.4 fusion.1
  29.0 1.9 %gather_fusion = bf16[16,128,128]{2,1,0:T(8,128)(2,1)S(1)} fusion(bf16[24,128,128]{2,1,0:T(8,128)(2,1)} %fusion.1, s32[1024]{0:T(1024)S(1)} %pad_clamp_fusion), kind=kCustom, calls=%fused_computation | custom fusion | bytes 1048640 | tf_op jit(solution)/shard_map/gather | solution.py:59
  30.9 3.9 %collective-permute-start.3 = (bf16[2,128,128]{2,1,0:T(8,128)(2,1)S(1)}, bf16[2,128,128]{2,1,0:T(8,128)(2,1)S(1)}, u32[]{:S(2)}, u32[]{:S(2)}) collective-permute-start(bf16[2,128,128]{2,1,0:T(8,128)(2,1)S(1)} %get-tuple-element.20), channel_id=1, source_target_pairs={{0,68},{4,72},{8,76},{12,80},{16,84},{20,88},{24,92},{28,96},{32,1... | collective-permute-start | bytes 196616 | tf_op jit(solution)/shard_map/ppermute | solution.py:23
  34.8 6.4 %collective-permute-start.4 = (bf16[2,128,128]{2,1,0:T(8,128)(2,1)S(1)}, bf16[2,128,128]{2,1,0:T(8,128)(2,1)S(1)}, u32[]{:S(2)}, u32[]{:S(2)}) collective-permute-start(bf16[2,128,128]{2,1,0:T(8,128)(2,1)S(1)} %get-tuple-element.19), channel_id=1, source_target_pairs={{0,64},{4,68},{8,72},{12,76},{16,80},{20,84},{24,88},{28,92},{32,9... | collective-permute-start | bytes 196616 | tf_op jit(solution)/shard_map/ppermute | solution.py:23
  41.2 6.9 %collective-permute-start.5 = (bf16[2,128,128]{2,1,0:T(8,128)(2,1)S(1)}, bf16[2,128,128]{2,1,0:T(8,128)(2,1)S(1)}, u32[]{:S(2)}, u32[]{:S(2)}) collective-permute-start(bf16[2,128,128]{2,1,0:T(8,128)(2,1)S(1)} %get-tuple-element.18), channel_id=1, source_target_pairs={{0,60},{4,64},{8,68},{12,72},{16,76},{20,80},{24,84},{28,88},{32,9... | collective-permute-start | bytes 196616 | tf_op jit(solution)/shard_map/ppermute | solution.py:23
  48.1 1.9 %collective-permute-start.6 = (bf16[2,128,128]{2,1,0:T(8,128)(2,1)S(1)}, bf16[2,128,128]{2,1,0:T(8,128)(2,1)S(1)}, u32[]{:S(2)}, u32[]{:S(2)}) collective-permute-start(bf16[2,128,128]{2,1,0:T(8,128)(2,1)S(1)} %get-tuple-element.17), channel_id=1, source_target_pairs={{0,4},{4,8},{8,12},{12,16},{16,20},{20,24},{24,28},{28,32},{32,36}... | collective-permute-start | bytes 196616 | tf_op jit(solution)/shard_map/ppermute | solution.py:23
  50.1 3.6 %collective-permute-start.7 = (bf16[2,128,128]{2,1,0:T(8,128)(2,1)S(1)}, bf16[2,128,128]{2,1,0:T(8,128)(2,1)S(1)}, u32[]{:S(2)}, u32[]{:S(2)}) collective-permute-start(bf16[2,128,128]{2,1,0:T(8,128)(2,1)S(1)} %get-tuple-element.16), channel_id=1, source_target_pairs={{4,0},{8,4},{12,8},{16,12},{20,16},{24,20},{28,24},{32,28},{36,32}... | collective-permute-start | bytes 196616 | tf_op jit(solution)/shard_map/ppermute | solution.py:23
  54.2 1.3 collective-permute-start.8
  55.5 1.3 collective-permute-start.9
  56.8 1.3 collective-permute-start.10
  58.2 3.9 %collective-permute-done.8 = bf16[2,128,128]{2,1,0:T(8,128)(2,1)S(1)} collective-permute-done((bf16[2,128,128]{2,1,0:T(8,128)(2,1)S(1)}, bf16[2,128,128]{2,1,0:T(8,128)(2,1)S(1)}, u32[]{:S(2)}, u32[]{:S(2)}) %collective-permute-start.8) | collective-permute-done | bytes 65568 | tf_op jit(solution)/shard_map/ppermute | solution.py:23
  62.1 6.8 %collective-permute-done.9 = bf16[2,128,128]{2,1,0:T(8,128)(2,1)S(1)} collective-permute-done((bf16[2,128,128]{2,1,0:T(8,128)(2,1)S(1)}, bf16[2,128,128]{2,1,0:T(8,128)(2,1)S(1)}, u32[]{:S(2)}, u32[]{:S(2)}) %collective-permute-start.9) | collective-permute-done | bytes 65568 | tf_op jit(solution)/shard_map/ppermute | solution.py:23
  71.6 30.8 %reduce-scatter.4.cloned.1.call-done = f32[32,1152]{1,0:T(8,128)} async-done(((f32[128,1152]{1,0:T(8,128)}), f32[32,1152]{1,0:T(8,128)}) %reduce-scatter.4.cloned.1.call-update) | async-done | bytes 147472 | tf_op jit(solution)/shard_map/reduce_scatter | solution.py:79
  102.4 1.2 copy.26
  104.5 58.9 %all-reduce.2.cloned.1.call-done = f32[32,1152]{0,1:T(8,128)} async-done(((f32[32,1152]{0,1:T(8,128)}), f32[32,1152]{0,1:T(8,128)}) %all-reduce.2.cloned.1.call-update) | async-done | bytes 147472 | tf_op jit(solution)/shard_map/psum | solution.py:28
  164.9 2.9 %cholesky.16 = f32[32,32]{1,0:T(8,128)S(1)} custom-call(f32[32,32]{1,0:T(8,128)S(1)} %fusion.16), custom_call_target="Cholesky" | custom-call | tf_op jit(solution)/shard_map/jit(cholesky)/cholesky | solution.py:89
  169.2 2.4 %custom-call.10 = f32[1,32,32]{1,2,0:T(8,128)S(1)} custom-call(f32[1,32,32]{2,1,0:T(8,128)S(1)} %fusion.11), custom_call_target="InvertDiagBlocksLowerTriangular" | custom-call | tf_op jit(solution)/shard_map/jit(_solve_triangular)/triangular_solve | solution.py:92
  171.9 1.8 fusion.12
  (66 shorter events, 14.5 us)
Async XLA Ops:
  7.2 11.8 %copy-start = (bf16[1,24,128,128]{3,2,1,0:T(8,128)(2,1)S(1)}, bf16[1,24,128,128]{3,2,1,0:T(8,128)(2,1)}, u32[]{:S(2)}) copy-start(bf16[1,24,128,128]{3,2,1,0:T(8,128)(2,1)} %param.7) | copy-start | bytes 2359300
  7.2 95.2 %reduce-scatter.4.cloned.1.call-start = ((), (), s32[]{:S(2)}) async-start(), calls=%async_computation.2 | async-start | bytes 737280 | tf_op jit(solution)/shard_map/reduce_scatter | solution.py:79
  8.1 17.3 %collective-permute-start = (bf16[128,128]{1,0:T(8,128)(2,1)S(1)}, bf16[128,128]{1,0:T(8,128)(2,1)S(1)}, u32[]{:S(2)}, u32[]{:S(2)}) collective-permute-start(bf16[128,128]{1,0:T(8,128)(2,1)S(1)} %get-tuple-element.12), channel_id=1, source_target_pairs={{1,0},{2,1},{3,2},{5,4},{6,5},{7,6},{9,8},{10,9},{11,10},{13,12},{... | collective-permute-start | bytes 98312 | tf_op jit(solution)/shard_map/ppermute | solution.py:15
  9.4 16.0 %collective-permute-start.2 = (bf16[128,128]{1,0:T(8,128)(2,1)S(1)}, bf16[128,128]{1,0:T(8,128)(2,1)S(1)}, u32[]{:S(2)}, u32[]{:S(2)}) collective-permute-start(bf16[128,128]{1,0:T(8,128)(2,1)S(1)} %get-tuple-element.11), channel_id=1, source_target_pairs={{0,1},{1,2},{2,3},{4,5},{5,6},{6,7},{8,9},{9,10},{10,11},{12,13},{... | collective-permute-start | bytes 98312 | tf_op jit(solution)/shard_map/ppermute | solution.py:12
  14.8 12.1 %collective-permute-start.1 = (bf16[128,128]{0,1:T(8,128)(2,1)S(1)}, bf16[128,128]{0,1:T(8,128)(2,1)S(1)}, u32[]{:S(2)}, u32[]{:S(2)}) collective-permute-start(bf16[128,128]{0,1:T(8,128)(2,1)S(1)} %bitcast.93), channel_id=1, source_target_pairs={{0,1},{1,2},{2,3},{4,5},{5,6},{6,7},{8,9},{9,10},{10,11},{12,13},{... | collective-permute-start | bytes 98312 | tf_op jit(solution)/shard_map/ppermute | solution.py:23
  19.0 1.6 copy-start.8
  19.0 1.7 copy-start.3
  20.5 3.4 %copy-start.1 = (bf16[1,3072,128]{2,1,0:T(8,128)(2,1)S(1)}, bf16[1,3072,128]{2,1,0:T(8,128)(2,1)}, u32[]{:S(2)}) copy-start(bf16[1,3072,128]{2,1,0:T(8,128)(2,1)} %param.6) | copy-start | bytes 2359300
  25.4 1.1 copy-start.4
  26.5 1.1 copy-start.5
  29.0 24.7 %copy-start.2 = (bf16[24,128,128]{2,1,0:T(8,128)(2,1)S(1)}, bf16[24,128,128]{2,1,0:T(8,128)(2,1)}, u32[]{:S(2)}) copy-start(bf16[24,128,128]{2,1,0:T(8,128)(2,1)} %fusion.1) | copy-start | bytes 2359300
  30.9 38.5 %copy-start.6 = (bf16[16,128,128]{2,1,0:T(8,128)(2,1)S(1)}, bf16[16,128,128]{2,1,0:T(8,128)(2,1)}, u32[]{:S(2)}) copy-start(bf16[16,128,128]{2,1,0:T(8,128)(2,1)} %gather_fusion.1) | copy-start | bytes 1572868
  30.9 23.2 %collective-permute-start.3 = (bf16[2,128,128]{2,1,0:T(8,128)(2,1)S(1)}, bf16[2,128,128]{2,1,0:T(8,128)(2,1)S(1)}, u32[]{:S(2)}, u32[]{:S(2)}) collective-permute-start(bf16[2,128,128]{2,1,0:T(8,128)(2,1)S(1)} %get-tuple-element.20), channel_id=1, source_target_pairs={{0,68},{4,72},{8,76},{12,80},{16,84},{20,88},{24,92},{28,96},{32,1... | collective-permute-start | bytes 196616 | tf_op jit(solution)/shard_map/ppermute | solution.py:23
  34.8 20.7 %collective-permute-start.4 = (bf16[2,128,128]{2,1,0:T(8,128)(2,1)S(1)}, bf16[2,128,128]{2,1,0:T(8,128)(2,1)S(1)}, u32[]{:S(2)}, u32[]{:S(2)}) collective-permute-start(bf16[2,128,128]{2,1,0:T(8,128)(2,1)S(1)} %get-tuple-element.19), channel_id=1, source_target_pairs={{0,64},{4,68},{8,72},{12,76},{16,80},{20,84},{24,88},{28,92},{32,9... | collective-permute-start | bytes 196616 | tf_op jit(solution)/shard_map/ppermute | solution.py:23
  41.2 15.6 %collective-permute-start.5 = (bf16[2,128,128]{2,1,0:T(8,128)(2,1)S(1)}, bf16[2,128,128]{2,1,0:T(8,128)(2,1)S(1)}, u32[]{:S(2)}, u32[]{:S(2)}) collective-permute-start(bf16[2,128,128]{2,1,0:T(8,128)(2,1)S(1)} %get-tuple-element.18), channel_id=1, source_target_pairs={{0,60},{4,64},{8,68},{12,72},{16,76},{20,80},{24,84},{28,88},{32,9... | collective-permute-start | bytes 196616 | tf_op jit(solution)/shard_map/ppermute | solution.py:23
  48.1 10.0 %collective-permute-start.6 = (bf16[2,128,128]{2,1,0:T(8,128)(2,1)S(1)}, bf16[2,128,128]{2,1,0:T(8,128)(2,1)S(1)}, u32[]{:S(2)}, u32[]{:S(2)}) collective-permute-start(bf16[2,128,128]{2,1,0:T(8,128)(2,1)S(1)} %get-tuple-element.17), channel_id=1, source_target_pairs={{0,4},{4,8},{8,12},{12,16},{16,20},{20,24},{24,28},{28,32},{32,36}... | collective-permute-start | bytes 196616 | tf_op jit(solution)/shard_map/ppermute | solution.py:23
  50.1 8.1 %collective-permute-start.7 = (bf16[2,128,128]{2,1,0:T(8,128)(2,1)S(1)}, bf16[2,128,128]{2,1,0:T(8,128)(2,1)S(1)}, u32[]{:S(2)}, u32[]{:S(2)}) collective-permute-start(bf16[2,128,128]{2,1,0:T(8,128)(2,1)S(1)} %get-tuple-element.16), channel_id=1, source_target_pairs={{4,0},{8,4},{12,8},{16,12},{20,16},{24,20},{28,24},{32,28},{36,32}... | collective-permute-start | bytes 196616 | tf_op jit(solution)/shard_map/ppermute | solution.py:23
  54.2 7.9 %collective-permute-start.8 = (bf16[2,128,128]{2,1,0:T(8,128)(2,1)S(1)}, bf16[2,128,128]{2,1,0:T(8,128)(2,1)S(1)}, u32[]{:S(2)}, u32[]{:S(2)}) collective-permute-start(bf16[2,128,128]{2,1,0:T(8,128)(2,1)S(1)} %get-tuple-element.15), channel_id=1, source_target_pairs={{60,0},{64,4},{68,8},{72,12},{76,16},{80,20},{84,24},{88,28},{92,3... | collective-permute-start | bytes 196616 | tf_op jit(solution)/shard_map/ppermute | solution.py:23
  55.5 13.4 %collective-permute-start.9 = (bf16[2,128,128]{2,1,0:T(8,128)(2,1)S(1)}, bf16[2,128,128]{2,1,0:T(8,128)(2,1)S(1)}, u32[]{:S(2)}, u32[]{:S(2)}) collective-permute-start(bf16[2,128,128]{2,1,0:T(8,128)(2,1)S(1)} %get-tuple-element.14), channel_id=1, source_target_pairs={{64,0},{68,4},{72,8},{76,12},{80,16},{84,20},{88,24},{92,28},{96,3... | collective-permute-start | bytes 196616 | tf_op jit(solution)/shard_map/ppermute | solution.py:23
  56.8 12.5 %collective-permute-start.10 = (bf16[2,128,128]{2,1,0:T(8,128)(2,1)S(1)}, bf16[2,128,128]{2,1,0:T(8,128)(2,1)S(1)}, u32[]{:S(2)}, u32[]{:S(2)}) collective-permute-start(bf16[2,128,128]{2,1,0:T(8,128)(2,1)S(1)} %get-tuple-element.13), channel_id=1, source_target_pairs={{68,0},{72,4},{76,8},{80,12},{84,16},{88,20},{92,24},{96,28},{100,... | collective-permute-start | bytes 196616 | tf_op jit(solution)/shard_map/ppermute | solution.py:23
  70.9 92.5 %all-reduce.2.cloned.1.call-start = ((), (), s32[]{:S(2)}) async-start(), calls=%async_computation.1 | async-start | bytes 1179648 | tf_op jit(solution)/shard_map/psum | solution.py:28
  102.4 71.3 %copy-start.7 = (f32[32,1152]{1,0:T(8,128)S(1)}, f32[32,1152]{1,0:T(8,128)}, u32[]{:S(2)}) copy-start(f32[32,1152]{1,0:T(8,128)} %reduce-scatter.4.cloned.1.call-done) | copy-start | bytes 442372
Sparse Core Ops, SparseCore 0:
  71.0 31.3 reduce-scatter.3
  104.7 58.6 all-reduce.1
where the time goes:
time: 184 us; the launch traced here: 183 us
  waiting for transfers between devices  101 us (55%)
  starting transfers between devices  36 us (20%)
  local copies, waits for them, and re-layouts  15.2 us (8%)
  between operations  15 us (8%)
  other arithmetic  9.15 us (5%)
  matrix products  6.45 us (4%)
    psum x1, waiting for transfers between devices, broadcast(): return lax.psum(jnp.where(mine, shard, jnp.zeros_like(shard)), axis)  58.9 us
    reduce_scatter x1, waiting for transfers between devices, per_device(): lax.psum_scatter(jnp.concatenate([gram_part[:, None, :], coupling], 1).re...  30.8 us
    ppermute x9, starting transfers between devices, shifted(): lax.ppermute(value, axis, [(source, source + steps) for source in range(i...  30.1 us
    ppermute x9, waiting for transfers between devices, shifted(): lax.ppermute(value, axis, [(source, source + steps) for source in range(i...  11.1 us
    unnamed x30, local copies, waits for them, and re-layouts  7.24 us
    ppermute x1, starting transfers between devices, padded_2(): lax.ppermute(lax.slice_in_dim(block, block.shape[dim] - width, None, axis...  4.55 us
  transfers between devices with their start and end apart: 13, of which 5 were waited for; matrix products, arithmetic and copies ran while one was open for 5% of the time, Pallas kernels for 0%

commit v1 on v0

--- a/solution.py
+++ b/solution.py
@@ -25,7 +25,7 @@
 
 def broadcast(shard, axis, root):
     mine = lax.axis_index(axis) == root
-    return lax.psum(jnp.where(mine, shard, jnp.zeros_like(shard)), axis)
+    return jnp.sum(lax.all_gather(jnp.where(mine, shard, jnp.zeros_like(shard)), axis), axis=0)
 
 
 def neighbour_offsets(across):

time: 184 us -> 134 us (0.73)
  the two profiles are of different devices: /device:TPU:2 before, /device:TPU:4 now
where the time goes in v1:
time: 134 us; the launch traced here: 133 us
  waiting for transfers between devices  42 us (31%)
  starting transfers between devices  36 us (27%)
  between operations  15 us (11%)
  local copies, waits for them, and re-layouts  13.3 us (10%)
  blocking collectives  12.9 us (10%)
  other arithmetic  8.67 us (6%)
  matrix products  5.02 us (4%)
    reduce_scatter x1, waiting for transfers between devices, per_device(): lax.psum_scatter(jnp.concatenate([gram_part[:, None, :], coupling], 1).re...  31.2 us
    ppermute x9, starting transfers between devices, shifted(): lax.ppermute(value, axis, [(source, source + steps) for source in range(i...  30.1 us
    all_gather x1, blocking collectives, broadcast(): lax.all_gather(jnp.where(mine, shard, jnp.zeros_like(shard)), axis)  12.9 us
    ppermute x9, waiting for transfers between devices, shifted(): lax.ppermute(value, axis, [(source, source + steps) for source in range(i...  10.8 us
    unnamed x29, local copies, waits for them, and re-layouts  5.03 us
    ppermute x1, starting transfers between devices, padded_2(): lax.ppermute(lax.slice_in_dim(block, block.shape[dim] - width, None, axis...  4.55 us
    another operation x3, other arithmetic, per_device(): factor = jnp.linalg.cholesky(pivot_block)  3.6 us
    another operation x2, other arithmetic, per_device(): jax.scipy.linalg.solve_triangular(factor, columns.T, lower=True)  3.09 us
  transfers between devices with their start and end apart: 12, of which 4 were waited for; matrix products, arithmetic and copies ran while one was open for 7% of the time, Pallas kernels for 0%

profile of v1, /device:TPU:4, one launch (start us, length us, event | category | flops | bytes accessed | tf_op | source)
XLA Modules:
  0.0 133.0 jit_solution(16932461411767773442)
XLA Ops:
  8.1 1.3 collective-permute-start
  9.4 4.5 %collective-permute-start.2 = (bf16[128,128]{1,0:T(8,128)(2,1)S(1)}, bf16[128,128]{1,0:T(8,128)(2,1)S(1)}, u32[]{:S(2)}, u32[]{:S(2)}) collective-permute-start(bf16[128,128]{1,0:T(8,128)(2,1)S(1)} %get-tuple-element.11), channel_id=1, source_target_pairs={{0,1},{1,2},{2,3},{4,5},{5,6},{6,7},{8,9},{9,10},{10,11},{12,13},{... | collective-permute-start | bytes 98312 | tf_op jit(solution)/shard_map/ppermute | solution.py:12
  14.8 3.5 %collective-permute-start.1 = (bf16[128,128]{0,1:T(8,128)(2,1)S(1)}, bf16[128,128]{0,1:T(8,128)(2,1)S(1)}, u32[]{:S(2)}, u32[]{:S(2)}) collective-permute-start(bf16[128,128]{0,1:T(8,128)(2,1)S(1)} %bitcast.94), channel_id=1, source_target_pairs={{0,1},{1,2},{2,3},{4,5},{5,6},{6,7},{8,9},{9,10},{10,11},{12,13},{... | collective-permute-start | bytes 98312 | tf_op jit(solution)/shard_map/ppermute | solution.py:23
  19.0 1.6 %fusion.7 = f32[24,128,128]{2,1,0:T(8,128)S(1)} fusion(bf16[24,128,128]{2,1,0:T(8,128)(2,1)} %bitcast.82, bf16[1,24,128,128]{3,2,1,0:T(8,128)(2,1)S(1)} %copy-done), kind=kOutput, calls=%fused_computation.15 | convolution fusion | flops 100663296 | bytes 3145728 | tf_op jit(solution)/shard_map/bij,bjk->bik/dot_general | solution.py:52
  21.6 2.3 %copy.25 = bf16[1,23,128,128]{2,3,1,0:T(8,128)(2,1)} copy(bf16[1,23,128,128]{3,2,1,0:T(8,128)(2,1)} %slice.98) | data formatting | bytes 1507328
  23.9 1.4 %gather_fusion.1 = bf16[16,128,128]{2,1,0:T(8,128)(2,1)} fusion(bf16[24,128,128]{2,1,0:T(8,128)(2,1)S(1)} %bitcast.83, s32[1024]{0:T(1024)S(1)} %pad_clamp_fusion), kind=kCustom, calls=%fused_computation.1 | custom fusion | bytes 1048640 | tf_op jit(solution)/shard_map/gather | solution.py:58
  25.4 1.0 copy-done.4
  27.6 1.4 %fusion.1 = bf16[24,128,128]{2,1,0:T(8,128)(2,1)} fusion(f32[24,128,128]{2,1,0:T(8,128)S(1)} %fusion.7, f32[24,128,128]{1,2,0:T(8,128)S(1)} %fusion.5, bf16[24,128,128]{2,1,0:T(8,128)(2,1)S(1)} %bitcast.87, bf16[23,128,128]{1,2,0:T(8,128)(2,1)S(1)} %bitcast.88, bf16[1,128,128]{1,2,0:T(8,128)(2,1)S(1)} %bitcast.93), kind=kOutput, calls=%fused_computation.5 | convolution fusion | flops 102236160 | bytes 5505024 | tf_op jit(solution)/shard_map/bji,bjk->bik/dot_general | solution.py:54
  29.0 1.9 %gather_fusion = bf16[16,128,128]{2,1,0:T(8,128)(2,1)S(1)} fusion(bf16[24,128,128]{2,1,0:T(8,128)(2,1)} %fusion.1, s32[1024]{0:T(1024)S(1)} %pad_clamp_fusion), kind=kCustom, calls=%fused_computation | custom fusion | bytes 1048640 | tf_op jit(solution)/shard_map/gather | solution.py:59
  30.9 3.9 %collective-permute-start.3 = (bf16[2,128,128]{2,1,0:T(8,128)(2,1)S(1)}, bf16[2,128,128]{2,1,0:T(8,128)(2,1)S(1)}, u32[]{:S(2)}, u32[]{:S(2)}) collective-permute-start(bf16[2,128,128]{2,1,0:T(8,128)(2,1)S(1)} %get-tuple-element.20), channel_id=1, source_target_pairs={{0,68},{4,72},{8,76},{12,80},{16,84},{20,88},{24,92},{28,96},{32,1... | collective-permute-start | bytes 196616 | tf_op jit(solution)/shard_map/ppermute | solution.py:23
  34.8 6.4 %collective-permute-start.4 = (bf16[2,128,128]{2,1,0:T(8,128)(2,1)S(1)}, bf16[2,128,128]{2,1,0:T(8,128)(2,1)S(1)}, u32[]{:S(2)}, u32[]{:S(2)}) collective-permute-start(bf16[2,128,128]{2,1,0:T(8,128)(2,1)S(1)} %get-tuple-element.19), channel_id=1, source_target_pairs={{0,64},{4,68},{8,72},{12,76},{16,80},{20,84},{24,88},{28,92},{32,9... | collective-permute-start | bytes 196616 | tf_op jit(solution)/shard_map/ppermute | solution.py:23
  41.2 6.9 %collective-permute-start.5 = (bf16[2,128,128]{2,1,0:T(8,128)(2,1)S(1)}, bf16[2,128,128]{2,1,0:T(8,128)(2,1)S(1)}, u32[]{:S(2)}, u32[]{:S(2)}) collective-permute-start(bf16[2,128,128]{2,1,0:T(8,128)(2,1)S(1)} %get-tuple-element.18), channel_id=1, source_target_pairs={{0,60},{4,64},{8,68},{12,72},{16,76},{20,80},{24,84},{28,88},{32,9... | collective-permute-start | bytes 196616 | tf_op jit(solution)/shard_map/ppermute | solution.py:23
  48.1 1.9 %collective-permute-start.6 = (bf16[2,128,128]{2,1,0:T(8,128)(2,1)S(1)}, bf16[2,128,128]{2,1,0:T(8,128)(2,1)S(1)}, u32[]{:S(2)}, u32[]{:S(2)}) collective-permute-start(bf16[2,128,128]{2,1,0:T(8,128)(2,1)S(1)} %get-tuple-element.17), channel_id=1, source_target_pairs={{0,4},{4,8},{8,12},{12,16},{16,20},{20,24},{24,28},{28,32},{32,36}... | collective-permute-start | bytes 196616 | tf_op jit(solution)/shard_map/ppermute | solution.py:23
  50.1 3.6 %collective-permute-start.7 = (bf16[2,128,128]{2,1,0:T(8,128)(2,1)S(1)}, bf16[2,128,128]{2,1,0:T(8,128)(2,1)S(1)}, u32[]{:S(2)}, u32[]{:S(2)}) collective-permute-start(bf16[2,128,128]{2,1,0:T(8,128)(2,1)S(1)} %get-tuple-element.16), channel_id=1, source_target_pairs={{4,0},{8,4},{12,8},{16,12},{20,16},{24,20},{28,24},{32,28},{36,32}... | collective-permute-start | bytes 196616 | tf_op jit(solution)/shard_map/ppermute | solution.py:23
  54.1 1.3 collective-permute-start.8
  55.5 1.3 collective-permute-start.9
  56.8 1.3 collective-permute-start.10
  58.2 3.8 %collective-permute-done.8 = bf16[2,128,128]{2,1,0:T(8,128)(2,1)S(1)} collective-permute-done((bf16[2,128,128]{2,1,0:T(8,128)(2,1)S(1)}, bf16[2,128,128]{2,1,0:T(8,128)(2,1)S(1)}, u32[]{:S(2)}, u32[]{:S(2)}) %collective-permute-start.8) | collective-permute-done | bytes 65568 | tf_op jit(solution)/shard_map/ppermute | solution.py:23
  61.9 6.9 %collective-permute-done.9 = bf16[2,128,128]{2,1,0:T(8,128)(2,1)S(1)} collective-permute-done((bf16[2,128,128]{2,1,0:T(8,128)(2,1)S(1)}, bf16[2,128,128]{2,1,0:T(8,128)(2,1)S(1)}, u32[]{:S(2)}, u32[]{:S(2)}) %collective-permute-start.9) | collective-permute-done | bytes 65568 | tf_op jit(solution)/shard_map/ppermute | solution.py:23
  69.5 1.1 copy.18
  71.2 31.2 %reduce-scatter.2.cloned.1.call-done = f32[32,1152]{1,0:T(8,128)} async-done(((f32[128,1152]{1,0:T(8,128)}), f32[32,1152]{1,0:T(8,128)}) %reduce-scatter.2.cloned.1.call-update) | async-done | bytes 147472 | tf_op jit(solution)/shard_map/reduce_scatter | solution.py:79
  103.4 12.9 %all-gather = f32[128,1152]{1,0:T(8,128)S(1)} all-gather(f32[32,1152]{1,0:T(8,128)S(1)} %broadcast_select_fusion), channel_id=2, replica_groups=mesh['sub'=128,'crow'=4] {'crow'}, dimensions={0}, use_global_device_ids=true | all-gather | bytes 737280 | tf_op jit(solution)/shard_map/all_gather | solution.py:28
  116.6 2.9 %cholesky.16 = f32[32,32]{1,0:T(8,128)S(1)} custom-call(f32[32,32]{1,0:T(8,128)S(1)} %fusion.16), custom_call_target="Cholesky" | custom-call | tf_op jit(solution)/shard_map/jit(cholesky)/cholesky | solution.py:89
  120.9 2.4 %custom-call.10 = f32[1,32,32]{1,2,0:T(8,128)S(1)} custom-call(f32[1,32,32]{2,1,0:T(8,128)S(1)} %fusion.11), custom_call_target="InvertDiagBlocksLowerTriangular" | custom-call | tf_op jit(solution)/shard_map/jit(_solve_triangular)/triangular_solve | solution.py:92
  (64 shorter events, 11.3 us)
Async XLA Ops:
  7.2 11.8 %copy-start = (bf16[1,24,128,128]{3,2,1,0:T(8,128)(2,1)S(1)}, bf16[1,24,128,128]{3,2,1,0:T(8,128)(2,1)}, u32[]{:S(2)}) copy-start(bf16[1,24,128,128]{3,2,1,0:T(8,128)(2,1)} %param.7) | copy-start | bytes 2359300
  7.2 95.2 %reduce-scatter.2.cloned.1.call-start = ((), (), s32[]{:S(2)}) async-start(), calls=%async_computation.1 | async-start | bytes 737280 | tf_op jit(solution)/shard_map/reduce_scatter | solution.py:79
  8.1 17.3 %collective-permute-start = (bf16[128,128]{1,0:T(8,128)(2,1)S(1)}, bf16[128,128]{1,0:T(8,128)(2,1)S(1)}, u32[]{:S(2)}, u32[]{:S(2)}) collective-permute-start(bf16[128,128]{1,0:T(8,128)(2,1)S(1)} %get-tuple-element.12), channel_id=1, source_target_pairs={{1,0},{2,1},{3,2},{5,4},{6,5},{7,6},{9,8},{10,9},{11,10},{13,12},{... | collective-permute-start | bytes 98312 | tf_op jit(solution)/shard_map/ppermute | solution.py:15
  9.4 16.0 %collective-permute-start.2 = (bf16[128,128]{1,0:T(8,128)(2,1)S(1)}, bf16[128,128]{1,0:T(8,128)(2,1)S(1)}, u32[]{:S(2)}, u32[]{:S(2)}) collective-permute-start(bf16[128,128]{1,0:T(8,128)(2,1)S(1)} %get-tuple-element.11), channel_id=1, source_target_pairs={{0,1},{1,2},{2,3},{4,5},{5,6},{6,7},{8,9},{9,10},{10,11},{12,13},{... | collective-permute-start | bytes 98312 | tf_op jit(solution)/shard_map/ppermute | solution.py:12
  14.8 12.0 %collective-permute-start.1 = (bf16[128,128]{0,1:T(8,128)(2,1)S(1)}, bf16[128,128]{0,1:T(8,128)(2,1)S(1)}, u32[]{:S(2)}, u32[]{:S(2)}) collective-permute-start(bf16[128,128]{0,1:T(8,128)(2,1)S(1)} %bitcast.94), channel_id=1, source_target_pairs={{0,1},{1,2},{2,3},{4,5},{5,6},{6,7},{8,9},{9,10},{10,11},{12,13},{... | collective-permute-start | bytes 98312 | tf_op jit(solution)/shard_map/ppermute | solution.py:23
  19.0 1.6 %copy-start.8 = (s32[1,8]{1,0:T(1,128)S(1)}, s32[1,8]{1,0:T(1,128)}, u32[]{:S(2)}) copy-start(s32[1,8]{1,0:T(1,128)} %param.10) | copy-start | bytes 100
  19.0 1.7 %copy-start.3 = (bf16[1,24,128,128]{3,2,1,0:T(8,128)(2,1)S(1)}, bf16[1,24,128,128]{3,2,1,0:T(8,128)(2,1)}, u32[]{:S(2)}) copy-start(bf16[1,24,128,128]{3,2,1,0:T(8,128)(2,1)} %param.8) | copy-start | bytes 2359300
  20.5 3.4 %copy-start.1 = (bf16[1,3072,128]{2,1,0:T(8,128)(2,1)S(1)}, bf16[1,3072,128]{2,1,0:T(8,128)(2,1)}, u32[]{:S(2)}) copy-start(bf16[1,3072,128]{2,1,0:T(8,128)(2,1)} %param.6) | copy-start | bytes 2359300
  25.3 1.1 copy-start.4
  26.5 1.1 copy-start.5
  29.0 24.7 %copy-start.2 = (bf16[24,128,128]{2,1,0:T(8,128)(2,1)S(1)}, bf16[24,128,128]{2,1,0:T(8,128)(2,1)}, u32[]{:S(2)}) copy-start(bf16[24,128,128]{2,1,0:T(8,128)(2,1)} %fusion.1) | copy-start | bytes 2359300
  30.9 38.1 %copy-start.6 = (bf16[16,128,128]{2,1,0:T(8,128)(2,1)S(1)}, bf16[16,128,128]{2,1,0:T(8,128)(2,1)}, u32[]{:S(2)}) copy-start(bf16[16,128,128]{2,1,0:T(8,128)(2,1)} %gather_fusion.1) | copy-start | bytes 1572868
  30.9 23.2 %collective-permute-start.3 = (bf16[2,128,128]{2,1,0:T(8,128)(2,1)S(1)}, bf16[2,128,128]{2,1,0:T(8,128)(2,1)S(1)}, u32[]{:S(2)}, u32[]{:S(2)}) collective-permute-start(bf16[2,128,128]{2,1,0:T(8,128)(2,1)S(1)} %get-tuple-element.20), channel_id=1, source_target_pairs={{0,68},{4,72},{8,76},{12,80},{16,84},{20,88},{24,92},{28,96},{32,1... | collective-permute-start | bytes 196616 | tf_op jit(solution)/shard_map/ppermute | solution.py:23
  34.8 20.6 %collective-permute-start.4 = (bf16[2,128,128]{2,1,0:T(8,128)(2,1)S(1)}, bf16[2,128,128]{2,1,0:T(8,128)(2,1)S(1)}, u32[]{:S(2)}, u32[]{:S(2)}) collective-permute-start(bf16[2,128,128]{2,1,0:T(8,128)(2,1)S(1)} %get-tuple-element.19), channel_id=1, source_target_pairs={{0,64},{4,68},{8,72},{12,76},{16,80},{20,84},{24,88},{28,92},{32,9... | collective-permute-start | bytes 196616 | tf_op jit(solution)/shard_map/ppermute | solution.py:23
  41.2 15.6 %collective-permute-start.5 = (bf16[2,128,128]{2,1,0:T(8,128)(2,1)S(1)}, bf16[2,128,128]{2,1,0:T(8,128)(2,1)S(1)}, u32[]{:S(2)}, u32[]{:S(2)}) collective-permute-start(bf16[2,128,128]{2,1,0:T(8,128)(2,1)S(1)} %get-tuple-element.18), channel_id=1, source_target_pairs={{0,60},{4,64},{8,68},{12,72},{16,76},{20,80},{24,84},{28,88},{32,9... | collective-permute-start | bytes 196616 | tf_op jit(solution)/shard_map/ppermute | solution.py:23
  48.1 10.0 %collective-permute-start.6 = (bf16[2,128,128]{2,1,0:T(8,128)(2,1)S(1)}, bf16[2,128,128]{2,1,0:T(8,128)(2,1)S(1)}, u32[]{:S(2)}, u32[]{:S(2)}) collective-permute-start(bf16[2,128,128]{2,1,0:T(8,128)(2,1)S(1)} %get-tuple-element.17), channel_id=1, source_target_pairs={{0,4},{4,8},{8,12},{12,16},{16,20},{20,24},{24,28},{28,32},{32,36}... | collective-permute-start | bytes 196616 | tf_op jit(solution)/shard_map/ppermute | solution.py:23
  50.1 8.1 %collective-permute-start.7 = (bf16[2,128,128]{2,1,0:T(8,128)(2,1)S(1)}, bf16[2,128,128]{2,1,0:T(8,128)(2,1)S(1)}, u32[]{:S(2)}, u32[]{:S(2)}) collective-permute-start(bf16[2,128,128]{2,1,0:T(8,128)(2,1)S(1)} %get-tuple-element.16), channel_id=1, source_target_pairs={{4,0},{8,4},{12,8},{16,12},{20,16},{24,20},{28,24},{32,28},{36,32}... | collective-permute-start | bytes 196616 | tf_op jit(solution)/shard_map/ppermute | solution.py:23
  54.1 7.8 %collective-permute-start.8 = (bf16[2,128,128]{2,1,0:T(8,128)(2,1)S(1)}, bf16[2,128,128]{2,1,0:T(8,128)(2,1)S(1)}, u32[]{:S(2)}, u32[]{:S(2)}) collective-permute-start(bf16[2,128,128]{2,1,0:T(8,128)(2,1)S(1)} %get-tuple-element.15), channel_id=1, source_target_pairs={{60,0},{64,4},{68,8},{72,12},{76,16},{80,20},{84,24},{88,28},{92,3... | collective-permute-start | bytes 196616 | tf_op jit(solution)/shard_map/ppermute | solution.py:23
  55.5 13.4 %collective-permute-start.9 = (bf16[2,128,128]{2,1,0:T(8,128)(2,1)S(1)}, bf16[2,128,128]{2,1,0:T(8,128)(2,1)S(1)}, u32[]{:S(2)}, u32[]{:S(2)}) collective-permute-start(bf16[2,128,128]{2,1,0:T(8,128)(2,1)S(1)} %get-tuple-element.14), channel_id=1, source_target_pairs={{64,0},{68,4},{72,8},{76,12},{80,16},{84,20},{88,24},{92,28},{96,3... | collective-permute-start | bytes 196616 | tf_op jit(solution)/shard_map/ppermute | solution.py:23
  56.8 12.2 %collective-permute-start.10 = (bf16[2,128,128]{2,1,0:T(8,128)(2,1)S(1)}, bf16[2,128,128]{2,1,0:T(8,128)(2,1)S(1)}, u32[]{:S(2)}, u32[]{:S(2)}) collective-permute-start(bf16[2,128,128]{2,1,0:T(8,128)(2,1)S(1)} %get-tuple-element.13), channel_id=1, source_target_pairs={{68,0},{72,4},{76,8},{80,12},{84,16},{88,20},{92,24},{96,28},{100,... | collective-permute-start | bytes 196616 | tf_op jit(solution)/shard_map/ppermute | solution.py:23
  102.4 21.2 %copy-start.7 = (f32[32,1152]{1,0:T(8,128)S(1)}, f32[32,1152]{1,0:T(8,128)}, u32[]{:S(2)}) copy-start(f32[32,1152]{1,0:T(8,128)} %reduce-scatter.2.cloned.1.call-done) | copy-start | bytes 442372
Sparse Core Ops, SparseCore 0:
  70.7 31.6 reduce-scatter.1
